TPU v7x, 512 devices: a whole 4x4x16 slice. The times are simulated.
512 devices in a mesh: section: 8 (over x, core), dp: 64 (over y, z).
Axes of the slice: x: 4, y: 4, z: 16, core: 2. Of those that a mesh axis runs over, the one named last changes fastest.
Arguments:
- activations: bfloat16 [8, 8192, 5120], P('section', 'dp'), may hold values from -200 to 200, as said below
- upstream: bfloat16 [8, 8192, 5120], P('section', 'dp'), may hold values from -120 to 120, as said below
- section_norm_gain: float32 [8, 5120], P('section'), may hold values from 0.1 to 1.9
- adapter_down_weight: bfloat16 [8, 16, 5120], P('section'), may hold values from -0.078125 to 0.078125
- adapter_up_weight: bfloat16 [8, 16, 5120], P('section'), may hold values from -0.078125 to 0.078125
Outputs:
- passed: bfloat16 [8, 8192, 5120], P('section', 'dp')
- grad_pair: bfloat16 [8, 163840], P('section', 'dp')
Inputs may be any that keep to these rules, and one draw needn't show every extreme that they name: `activations`: activations of one token position share a part across replicas; rows and features have different scales. `upstream`: gradients of one token position share a part across replicas.
All inputs are finite; a program needn't handle non-finite values.
Results may differ from a plain program's by a relative error of at most 0.0034.
Values may be sent and summed in bfloat16 or wider, within the bound.
No kernel may reach another device: no remote copies, remote signals or barrier semaphores. Data moves between devices by JAX's collectives and lax.ppermute only.
A program may use at most 64 MiB of HBM per device.

v0:
```python
import jax
import jax.numpy as jnp
from jax import lax
from jax.sharding import PartitionSpec as P

norm_eps = 1e-05
pair_eps = 1e-06
adapter_scale = 2.0
HIGH = lax.Precision.HIGHEST


def from_behind(x, axis, by):
    size = lax.axis_size(axis)
    pairs = [(i, i + by) for i in range(size) if 0 <= i + by < size]
    return lax.ppermute(x, axis, pairs)


def replica_backward(inputs, incoming_gradient, gain_row, down_rows, upward_rows):
    widened = inputs.astype(jnp.float32)
    inverse = lax.rsqrt(jnp.mean(widened * widened, axis=-1, keepdims=True) + norm_eps)
    scaled = widened * inverse
    normed = (scaled * gain_row).astype(jnp.bfloat16)
    reduced_gradient = jnp.einsum(
        "sh,gh->sg", normed, down_rows, preferred_element_type=jnp.float32
    ).astype(jnp.bfloat16)
    count_of_rows = inputs.shape[0]
    upward_term = (
        adapter_scale
        * jnp.einsum(
            "tk,td->kd", reduced_gradient, incoming_gradient, preferred_element_type=jnp.float32
        )
        / count_of_rows
    )
    backward_lowrank = (
        adapter_scale
        * jnp.einsum(
            "sh,gh->sg", incoming_gradient, upward_rows, preferred_element_type=jnp.float32
        )
    ).astype(jnp.bfloat16)
    down_term = (
        jnp.einsum("tk,td->kd", backward_lowrank, normed, preferred_element_type=jnp.float32)
        / count_of_rows
    )
    back_norm = (
        jnp.einsum("tk,kd->td", backward_lowrank, down_rows, preferred_element_type=jnp.float32)
        * gain_row
    )
    centre = jnp.mean(back_norm * scaled, axis=-1, keepdims=True)
    passed = incoming_gradient.astype(jnp.float32) + inverse * (back_norm - scaled * centre)
    return (passed.astype(jnp.bfloat16), jnp.stack([down_term, upward_term]))


def swap_rows(c, level_bit):
    t, n = (c.shape[0], c.shape[1])
    rest = c.shape[2:]
    g = c.reshape((t, n // 2 ** (level_bit + 1), 2, 2**level_bit) + rest)
    return g[:, :, ::-1].reshape(c.shape)


def coefficient_tree(gram):
    tensors, n = (gram.shape[0], gram.shape[1])
    coef = jnp.broadcast_to(jnp.eye(n, dtype=jnp.float32), (tensors, n, n))
    for level_bit in range(n.bit_length() - 1):
        partner = swap_rows(coef, level_bit)
        gc = jnp.einsum("tra,tab->trb", coef, gram, precision=HIGH)
        inner_sum = jnp.sum(gc * partner, axis=-1, keepdims=True)
        own_square = jnp.sum(gc * coef, axis=-1, keepdims=True)
        far_square = swap_rows(own_square, level_bit)
        keep_coef = 1.0 - inner_sum / (2.0 * (own_square + pair_eps))
        take_coef = 1.0 - inner_sum / (2.0 * (far_square + pair_eps))
        coef = keep_coef * coef + take_coef * partner
    return coef[:, 0, :]


def gram_adasum(grad_pair):
    devices = lax.axis_size("dp")
    me = lax.axis_index("dp")
    flat = grad_pair.reshape(devices, -1)
    chunks = lax.all_to_all(flat, "dp", 0, 0, tiled=True)
    tensors = grad_pair.shape[0]
    per_tensor = devices // tensors
    mine = me // per_tensor
    partial = jnp.dot(chunks, chunks.T, precision=HIGH, preferred_element_type=jnp.float32)
    slot = (jnp.arange(tensors) == mine)[:, None, None]
    gram = lax.psum(jnp.where(slot, partial[None], 0.0), "dp")
    coef = coefficient_tree(gram)
    own_coef = jnp.sum(jnp.where((jnp.arange(tensors) == mine)[:, None], coef, 0.0), axis=0)
    combined = jnp.sum(own_coef[:, None] * chunks, axis=0)
    return combined.astype(jnp.bfloat16)[None]


def per_device(activations, upstream, section_norm_gain, adapter_down_weight, adapter_up_weight):
    passed_local, grad_pair = replica_backward(
        activations[0],
        upstream[0],
        section_norm_gain[0],
        adapter_down_weight[0],
        adapter_up_weight[0],
    )
    shifted = from_behind(passed_local[None], "section", -1)
    merged_gradient = gram_adasum(grad_pair)
    return (shifted, merged_gradient)


def solution(mesh):
    return jax.shard_map(
        per_device,
        mesh=mesh,
        in_specs=(
            P("section", "dp", None),
            P("section", "dp", None),
            P("section", None),
            P("section", None, None),
            P("section", None, None),
        ),
        out_specs=(P("section", "dp", None), P("section", "dp")),
        check_vma=False,
    )
```

profile of v0, /device:TPU:6, one launch (start us, length us, event | category | flops | bytes accessed | tf_op | source)
XLA Modules:
  0.0 352.2 jit_solution(4884689482944939448)
XLA Ops:
  0.7 1.8 fusion.13
  2.5 1.8 fusion.31
  4.3 1.9 fusion
  6.2 0.5 fusion.1
  6.7 0.5 copy-done.3
  7.2 1.6 all_to_all.11
  8.8 18.7 %all-to-all-start = ((f32[64,1,2560]{2,1,0:T(1,128)}), f32[64,1,2560]{2,1,0:T(1,128)S(1)}, u32[]{:S(2)}, u32[]{:S(2)}) async-start(f32[64,1,2560]{2,1,0:T(1,128)} %all_to_all.11), calls=%async_computation | async-start | bytes 1310720 | tf_op jit(solution)/shard_map/all_to_all | solution.py:79
  27.5 0.7 fusion.7
  28.2 1.9 fusion.20
  30.1 1.9 collective-permute-start
  32.6 0.1 fusion.59
  32.7 0.1 compare_convert_fusion
  32.8 14.6 %collective-permute-done = bf16[1,128,5120]{2,1,0:T(8,128)(2,1)S(1)} collective-permute-done((bf16[1,128,5120]{2,1,0:T(8,128)(2,1)}, bf16[1,128,5120]{2,1,0:T(8,128)(2,1)S(1)}, u32[]{:S(2)}, u32[]{:S(2)}) %collective-permute-start) | collective-permute-done | bytes 1310752 | tf_op jit(solution)/shard_map/ppermute | solution.py:15
  47.5 17.5 %all-to-all-done = f32[64,1,2560]{2,1,0:T(1,128)S(1)} async-done(((f32[64,1,2560]{2,1,0:T(1,128)}), f32[64,1,2560]{2,1,0:T(1,128)S(1)}, u32[]{:S(2)}, u32[]{:S(2)}) %all-to-all-start) | async-done | bytes 655392 | tf_op jit(solution)/shard_map/all_to_all | solution.py:79
  64.9 0.7 fusion.39
  65.7 274.8 %psum.7 = f32[2,64,64]{1,2,0:T(8,128)S(1)} all-reduce(f32[2,64,64]{1,2,0:T(8,128)S(1)} %broadcast_select_fusion), channel_id=1, replica_groups=mesh['section'=8,'dp'=64] {'dp'}, use_global_device_ids=true, to_apply=%region_2.3 | all-reduce | flops 8192 | bytes 65536 | tf_op jit(solution)/shard_map/psum | solution.py:85
  340.5 0.2 multiply_reduce_fusion.10
  340.7 0.1 reduce_sum.178
  340.9 0.1 reduce_sum.182
  341.0 0.1 reshape_broadcast_in_dim.18
  341.2 0.1 mul.669
  341.3 0.1 mul.672
  341.4 0.1 mul.689
  341.6 0.1 copy.128
  341.7 0.1 copy.129
  341.8 0.1 copy.133
  341.9 0.1 copy.134
  342.0 0.1 copy.130
  342.1 0.2 multiply_add_fusion.6
  342.3 0.2 rev.38
  342.7 0.2 multiply_reduce_fusion.8
  342.9 0.1 reshape_broadcast_in_dim.19
  343.1 0.1 reshape.734
  343.2 0.1 mul.684
  343.3 0.1 reduce_sum.181
  343.5 0.1 mul.687
  343.6 0.2 fusion.50
  344.0 0.2 multiply_reduce_fusion.6
  344.2 0.1 reshape_broadcast_in_dim.20
  344.4 0.1 mul.705
  344.5 0.1 mul.723
  344.6 0.1 mul.712
  344.8 0.1 reduce_sum.186
  344.9 0.1 mul.719
  345.1 0.1 reduce_sum.185
  345.3 0.2 multiply_add_fusion.3
  345.6 0.2 multiply_reduce_fusion.4
  345.9 0.1 reshape_broadcast_in_dim.21
  346.0 0.1 mul.732
  346.3 0.1 mul.752
  346.6 0.1 mul.744
  346.8 0.1 mul.748
  347.2 0.2 multiply_add_fusion.1
  347.6 0.2 multiply_reduce_fusion.2
  348.5 0.1 mul.787
  348.7 0.1 mul.779
  348.9 0.1 mul.783
  349.3 0.2 fusion.49
  349.7 0.2 multiply_reduce_fusion
  350.2 0.1 fusion.48
  350.3 0.1 select_reduce_fusion
  350.4 0.1 fusion.41
  350.5 0.6 convert_element_type.85
  351.1 1.1 copy.181
  (103 shorter events, 4.3 us)
Async XLA Ops:
  0.6 3.6 %copy-start = (bf16[1,16,5120]{2,1,0:T(8,128)(2,1)S(1)}, bf16[1,16,5120]{2,1,0:T(8,128)(2,1)}, u32[]{:S(2)}) copy-start(bf16[1,16,5120]{2,1,0:T(8,128)(2,1)} %param.8) | copy-start | bytes 491524
  0.6 3.6 %copy-start.1 = (bf16[1,128,5120]{2,1,0:T(8,128)(2,1)S(1)}, bf16[1,128,5120]{2,1,0:T(8,128)(2,1)}, u32[]{:S(2)}) copy-start(bf16[1,128,5120]{2,1,0:T(8,128)(2,1)} %param.5) | copy-start | bytes 3932164
  0.7 3.6 %copy-start.2 = (bf16[1,128,5120]{2,1,0:T(8,128)(2,1)S(1)}, bf16[1,128,5120]{2,1,0:T(8,128)(2,1)}, u32[]{:S(2)}) copy-start(bf16[1,128,5120]{2,1,0:T(8,128)(2,1)} %param.6) | copy-start | bytes 3932164
  0.7 3.6 %copy-start.4 = (f32[1,5120]{1,0:T(1,128)S(1)}, f32[1,5120]{1,0:T(1,128)}, u32[]{:S(2)}) copy-start(f32[1,5120]{1,0:T(1,128)} %param.7) | copy-start | bytes 61444
  6.2 1.0 copy-start.3
  8.8 56.1 %all-to-all-start = ((f32[64,1,2560]{2,1,0:T(1,128)}), f32[64,1,2560]{2,1,0:T(1,128)S(1)}, u32[]{:S(2)}, u32[]{:S(2)}) async-start(f32[64,1,2560]{2,1,0:T(1,128)} %all_to_all.11), calls=%async_computation | async-start | bytes 1310720 | tf_op jit(solution)/shard_map/all_to_all | solution.py:79
  30.1 17.3 %collective-permute-start = (bf16[1,128,5120]{2,1,0:T(8,128)(2,1)}, bf16[1,128,5120]{2,1,0:T(8,128)(2,1)S(1)}, u32[]{:S(2)}, u32[]{:S(2)}) collective-permute-start(bf16[1,128,5120]{2,1,0:T(8,128)(2,1)} %fusion.20), channel_id=1, source_target_pairs={{64,0},{128,64},{192,128},{256,192},{320,256},{384,320},{448,384},... | collective-permute-start | bytes 3932168 | tf_op jit(solution)/shard_map/ppermute | solution.py:15
where the time goes:
time: 352 us
  blocking collectives  275 us (78%)
  waiting for transfers between devices  32.1 us (9%)
  starting transfers between devices  20.6 us (6%)
  local copies, waits for them, and re-layouts  10.4 us (3%)
  matrix products  6.79 us (2%)
  other arithmetic  6.14 us (2%)
    psum x1, blocking collectives, gram_adasum(): gram = lax.psum(jnp.where(slot, partial[None], 0.0), 'dp')  275 us
    all_to_all x1, starting transfers between devices, gram_adasum(): chunks = lax.all_to_all(flat, 'dp', 0, 0, tiled=True)  18.7 us
    all_to_all x1, waiting for transfers between devices, gram_adasum(): chunks = lax.all_to_all(flat, 'dp', 0, 0, tiled=True)  17.5 us
    ppermute x1, waiting for transfers between devices, from_behind(): return lax.ppermute(x, axis, pairs)  14.6 us
  transfers between devices with their start and end apart: 2, of which 2 were waited for; matrix products, arithmetic and copies ran while one was open for 1% of the time, Pallas kernels for 0%

commit v1 on v0

--- a/solution.py
+++ b/solution.py
@@ -82,7 +82,8 @@
     mine = me // per_tensor
     partial = jnp.dot(chunks, chunks.T, precision=HIGH, preferred_element_type=jnp.float32)
     slot = (jnp.arange(tensors) == mine)[:, None, None]
-    gram = lax.psum(jnp.where(slot, partial[None], 0.0), "dp")
+    _switch_modes = lambda v0: jnp.sum(jax.lax.all_gather(v0, "dp"), axis=0)
+    gram = _switch_modes(jnp.where(slot, partial[None], 0.0))
     coef = coefficient_tree(gram)
     own_coef = jnp.sum(jnp.where((jnp.arange(tensors) == mine)[:, None], coef, 0.0), axis=0)
     combined = jnp.sum(own_coef[:, None] * chunks, axis=0)

time: 352 us -> 235 us (0.67)
  blocking collectives: 275 us -> 0 us
  waiting for transfers between devices: 32.1 us -> 171 us
  between operations: 1.28 us -> 14.7 us
  other arithmetic: 6.14 us -> 10.4 us
    psum x1 -> x0, blocking collectives: 275 us -> none  [gram_adasum(): gram = lax.psum(jnp.where(slot, partial[None], 0.0), 'dp')]
    all_gather x0 -> x1, waiting for transfers between devices: none -> 119 us  [gram_adasum(): _switch_modes = lambda v0: jnp.sum(jax.lax.all_gather(v0, 'dp'), axis=0)]
    all_to_all x1, waiting for transfers between devices: 17.5 us -> 37.3 us  [gram_adasum(): chunks = lax.all_to_all(flat, 'dp', 0, 0, tiled=True)]
  transfers between devices with their start and end apart: 2 -> 3, of which waited for: 2 -> 3; matrix products, arithmetic and copies ran while one was open for 1% -> 1% of each run, Pallas kernels for 0% -> 0%
where the time goes in v1:
time: 235 us; the launch traced here: 234 us
  waiting for transfers between devices  171 us (73%)
  starting transfers between devices  20.7 us (9%)
  between operations  14.7 us (6%)
  other arithmetic  10.4 us (4%)
  local copies, waits for them, and re-layouts  9.89 us (4%)
  matrix products  7.97 us (3%)
    all_gather x1, waiting for transfers between devices, gram_adasum(): _switch_modes = lambda v0: jnp.sum(jax.lax.all_gather(v0, 'dp'), axis=0)  119 us
    all_to_all x1, waiting for transfers between devices, gram_adasum(): chunks = lax.all_to_all(flat, 'dp', 0, 0, tiled=True)  37.3 us
    all_to_all x1, starting transfers between devices, gram_adasum(): chunks = lax.all_to_all(flat, 'dp', 0, 0, tiled=True)  18.7 us
    ppermute x1, waiting for transfers between devices, from_behind(): return lax.ppermute(x, axis, pairs)  14.7 us
  transfers between devices with their start and end apart: 3, of which 3 were waited for; matrix products, arithmetic and copies ran while one was open for 1% of the time, Pallas kernels for 0%

profile of v1, /device:TPU:6, one launch (start us, length us, event | category | flops | bytes accessed | tf_op | source)
XLA Modules:
  0.0 234.2 jit_solution(15056871511195180932)
XLA Ops:
  7.2 1.8 fusion.13
  9.0 1.8 fusion.31
  10.8 1.2 fusion.1
  12.0 1.9 fusion
  13.9 1.1 pad_maximum_fusion
  15.0 1.6 all_to_all.11
  16.6 18.7 %all-to-all-start = ((f32[64,1,2560]{2,1,0:T(1,128)}), f32[64,1,2560]{2,1,0:T(1,128)S(1)}, u32[]{:S(2)}, u32[]{:S(2)}) async-start(f32[64,1,2560]{2,1,0:T(1,128)} %all_to_all.11), calls=%async_computation | async-start | bytes 1310720 | tf_op jit(solution)/shard_map/all_to_all | solution.py:79
  35.4 37.3 %all-to-all-done = f32[64,1,2560]{2,1,0:T(1,128)S(1)} async-done(((f32[64,1,2560]{2,1,0:T(1,128)}), f32[64,1,2560]{2,1,0:T(1,128)S(1)}, u32[]{:S(2)}, u32[]{:S(2)}) %all-to-all-start) | async-done | bytes 655392 | tf_op jit(solution)/shard_map/all_to_all | solution.py:79
  72.8 0.7 fusion.39
  73.4 0.7 broadcast_select_fusion
  74.2 0.7 fusion.7
  74.8 1.9 fusion.20
  76.7 1.9 collective-permute-start
  79.2 0.1 fusion.59
  79.3 0.1 compare_convert_fusion
  79.4 14.7 %collective-permute-done = bf16[1,128,5120]{2,1,0:T(8,128)(2,1)S(1)} collective-permute-done((bf16[1,128,5120]{2,1,0:T(8,128)(2,1)}, bf16[1,128,5120]{2,1,0:T(8,128)(2,1)S(1)}, u32[]{:S(2)}, u32[]{:S(2)}) %collective-permute-start) | collective-permute-done | bytes 1310752 | tf_op jit(solution)/shard_map/ppermute | solution.py:15
  94.1 118.6 %all-gather.2.cloned.1.call-done = f32[64,2,64,64]{3,2,1,0:T(8,128)} async-done(((f32[1,2,64,64]{3,2,1,0:T(8,128)}), f32[64,2,64,64]{3,2,1,0:T(8,128)}) %all-gather.2.cloned.1.call-update) | async-done | bytes 2097168 | tf_op jit(solution)/shard_map/all_gather | solution.py:85
  212.7 2.6 %reduce_sum.185 = f32[2,64,64]{2,1,0:T(8,128)S(1)} reduce(f32[64,2,64,64]{3,2,1,0:T(8,128)} %all-gather.2.cloned.1.call-done, f32[]{:T(128)} %constant.38.clone.1), dimensions={0}, to_apply=%region_2.3 | reduce | flops 516096 | bytes 2129924 | tf_op jit(solution)/shard_map/reduce_sum | solution.py:85
  215.2 0.3 multiply_reduce_fusion.10
  215.5 0.1 reshape_broadcast_in_dim.18
  215.7 0.1 mul.669
  215.8 0.1 reduce_sum.188
  216.0 0.1 mul.672
  216.1 0.1 copy.168
  216.2 0.1 copy.172
  216.3 0.1 copy.167
  216.5 0.1 copy.169
  216.6 0.1 copy.173
  216.7 0.2 multiply_add_fusion.6
  216.9 0.2 rev.38
  217.2 0.3 multiply_reduce_fusion.8
  217.5 0.1 reshape_broadcast_in_dim.19
  217.7 0.1 mul.684
  217.8 0.1 mul.748
  218.0 0.1 mul.744
  218.4 0.1 mul.687
  218.5 0.1 reshape.737
  218.6 0.1 reduce_sum.191
  218.7 0.1 mul.689
  218.9 0.1 reduce_sum.192
  219.0 0.2 fusion.50
  219.4 0.3 multiply_reduce_fusion.6
  219.7 0.1 reshape_broadcast_in_dim.20
  219.8 0.1 mul.705
  219.9 0.1 mul.752
  220.1 0.1 mul.719
  220.3 0.1 mul.712
  220.5 0.1 reduce_sum.197
  220.9 0.1 mul.723
  221.1 0.2 multiply_add_fusion.3
  221.4 0.3 multiply_reduce_fusion.4
  221.8 0.1 mul.732
  222.1 0.1 mul.783
  222.4 0.1 mul.779
  222.6 0.1 mul.787
  223.3 0.2 multiply_add_fusion.1
  223.6 0.3 multiply_reduce_fusion.2
  224.5 0.2 fusion.49
  224.8 0.3 multiply_reduce_fusion
  225.4 0.1 fusion.48
  225.5 0.1 select_reduce_fusion
  225.6 0.1 fusion.41
  225.7 0.6 convert_element_type.85
  226.3 1.1 copy.229
  (104 shorter events, 4.4 us)
Async XLA Ops:
  7.2 4.9 %copy-start = (bf16[1,16,5120]{2,1,0:T(8,128)(2,1)S(1)}, bf16[1,16,5120]{2,1,0:T(8,128)(2,1)}, u32[]{:S(2)}) copy-start(bf16[1,16,5120]{2,1,0:T(8,128)(2,1)} %param.8) | copy-start | bytes 491524
  7.2 3.6 %copy-start.1 = (bf16[1,128,5120]{2,1,0:T(8,128)(2,1)S(1)}, bf16[1,128,5120]{2,1,0:T(8,128)(2,1)}, u32[]{:S(2)}) copy-start(bf16[1,128,5120]{2,1,0:T(8,128)(2,1)} %param.5) | copy-start | bytes 3932164
  7.2 4.8 %copy-start.2 = (bf16[1,128,5120]{2,1,0:T(8,128)(2,1)S(1)}, bf16[1,128,5120]{2,1,0:T(8,128)(2,1)}, u32[]{:S(2)}) copy-start(bf16[1,128,5120]{2,1,0:T(8,128)(2,1)} %param.6) | copy-start | bytes 3932164
  7.2 3.6 %copy-start.3 = (f32[1,5120]{1,0:T(1,128)S(1)}, f32[1,5120]{1,0:T(1,128)}, u32[]{:S(2)}) copy-start(f32[1,5120]{1,0:T(1,128)} %param.7) | copy-start | bytes 61444
  16.6 56.1 %all-to-all-start = ((f32[64,1,2560]{2,1,0:T(1,128)}), f32[64,1,2560]{2,1,0:T(1,128)S(1)}, u32[]{:S(2)}, u32[]{:S(2)}) async-start(f32[64,1,2560]{2,1,0:T(1,128)} %all_to_all.11), calls=%async_computation | async-start | bytes 1310720 | tf_op jit(solution)/shard_map/all_to_all | solution.py:79
  35.4 177.3 %all-gather.2.cloned.1.call-start = ((), (), s32[]{:S(2)}) async-start(), calls=%async_computation.1 | async-start | bytes 4259840 | tf_op jit(solution)/shard_map/all_gather | solution.py:85
  76.7 17.3 %collective-permute-start = (bf16[1,128,5120]{2,1,0:T(8,128)(2,1)}, bf16[1,128,5120]{2,1,0:T(8,128)(2,1)S(1)}, u32[]{:S(2)}, u32[]{:S(2)}) collective-permute-start(bf16[1,128,5120]{2,1,0:T(8,128)(2,1)} %fusion.20), channel_id=1, source_target_pairs={{64,0},{128,64},{192,128},{256,192},{320,256},{384,320},{448,384},... | collective-permute-start | bytes 3932168 | tf_op jit(solution)/shard_map/ppermute | solution.py:15
Sparse Core Ops, SparseCore 0:
  74.3 138.3 all-gather.1
